TPU v7x, 512 devices: a whole 4x4x16 slice. The times are simulated.
512 devices in a mesh: blk: 32 (over z, core), col: 16 (over y, x).
Axes of the slice: x: 4, y: 4, z: 16, core: 2. Of those that a mesh axis runs over, the one named last changes fastest.
Arguments:
- density: float32 [96, 7, 256, 256], P('blk', None, 'col'), as said below
- band_widths: int32 [96], P('blk'), may hold values from 1 to 3, as said below
Outputs:
- purified: float32 [96, 7, 256, 256], P('blk', None, 'col')
Inputs may be any that keep to these rules, and one draw needn't show every extreme that they name: `band_widths`: each block row keeps between 1 and 3 blocks on each side; 3 is reached in every draw. `density`: diagonal entries of the diagonal blocks lie between 0.05 and 0.95, all other entries are small.
All inputs are finite; a program needn't handle non-finite values.
Results may differ from a plain program's by a relative error of at most 0.00013.
Values sent between devices are 32-bit elements; how exact they have to be, the bound alone decides.
No kernel may reach another device: no remote copies, remote signals or barrier semaphores. Data moves between devices by JAX's collectives and lax.ppermute only.
A program may use at most 64 MiB of HBM per device.

v0:
```python
import jax
import jax.numpy as jnp
from jax import lax
from jax.sharding import PartitionSpec as P

W = 3


def send(cells, shift):
    count = lax.axis_size("blk")
    return lax.ppermute(cells, "blk", [(i, (i + shift) % count) for i in range(count)])


def halo_pieces(cells):
    rows = cells.shape[0]
    tail = [cells[rows - W + k, W - k :] for k in range(W)]
    head = [cells[k, : 2 * W - k] for k in range(W)]
    return (tail, head)


def extend(right):
    tail, head = halo_pieces(right)
    from_left = send(jnp.concatenate(tail, axis=0), 1)
    from_right = send(jnp.concatenate(head, axis=0), -1)
    zero = jnp.zeros((1,) + right.shape[2:], right.dtype)
    rows = []
    start = 0
    for k in range(W):
        width = 2 * W + 1 - (W - k)
        piece = from_left[start : start + width]
        start += width
        rows.append(
            jnp.concatenate([jnp.broadcast_to(zero, (W - k,) + right.shape[2:]), piece], axis=0)
        )
    left = jnp.stack(rows)
    rows = []
    start = 0
    for k in range(W):
        width = 2 * W - k
        piece = from_right[start : start + width]
        start += width
        rows.append(
            jnp.concatenate([piece, jnp.broadcast_to(zero, (k + 1,) + right.shape[2:])], axis=0)
        )
    right_rows = jnp.stack(rows)
    return jnp.concatenate([left, right, right_rows], axis=0)


def contract(extended, shard_rows, keep=None):
    local_rows = shard_rows.shape[0]
    span = 2 * W + 1
    zeros = jnp.zeros_like(extended[:local_rows, :1])
    shifted = []
    for inner_band in range(span):
        window = extended[inner_band : inner_band + local_rows]
        shift = inner_band - W
        if shift > 0:
            window = jnp.concatenate([zeros] * shift + [window[:, : span - shift]], axis=1)
        elif shift < 0:
            window = jnp.concatenate([window[:, -shift:]] + [zeros] * -shift, axis=1)
        shifted.append(window)
    stacked = jnp.stack(shifted, axis=3)
    if keep is not None:
        shard_rows = shard_rows * keep
    return jnp.einsum("ibcas,iasr->ibcr", stacked, shard_rows, precision=lax.Precision.HIGH)


def on_device(density, band_widths):
    offsets = jnp.abs(jnp.arange(2 * W + 1, dtype=jnp.int32) - W)
    pattern = (offsets[None, :] <= band_widths[:, None]).astype(jnp.float32)[:, :, None, None]
    current = density * pattern
    for purify_step in range(2):
        if purify_step == 0:
            gathered, keep = (lax.all_gather(density, "col", axis=2, tiled=True), pattern)
        else:
            gathered, keep = (lax.all_gather(current, "col", axis=2, tiled=True), None)
        square = contract(extend(current), gathered, keep) * pattern
        third_power = contract(extend(square), gathered, keep) * pattern
        current = 3.0 * square - 2.0 * third_power
    return current


def solution(mesh):
    in_specs = (P("blk", None, "col", None), P("blk"))
    out_specs = P("blk", None, "col", None)
    return jax.shard_map(
        on_device, mesh=mesh, in_specs=in_specs, out_specs=out_specs, check_vma=False
    )
```

profile of v0, /device:TPU:97, one launch (start us, length us, event | category | flops | bytes accessed | tf_op | source)
XLA Modules:
  0.0 198.5 jit_solution(10707903417032842990)
XLA Ops:
  6.5 0.0 all-gather.3.cloned.1.call-start
  6.5 0.7 all-gather.3.cloned.1.call-update
  7.3 0.0 all-gather.5.cloned.1.call-start
  7.3 0.7 compare_convert_fusion
  8.0 1.1 broadcast_multiply_fusion
  9.2 0.0 copy-start.2
  9.2 3.4 %collective-permute-start = (f32[15,16,256]{2,1,0:T(8,128)S(1)}, f32[15,16,256]{2,1,0:T(8,128)S(1)}, u32[]{:S(2)}, u32[]{:S(2)}) collective-permute-start(f32[15,16,256]{2,1,0:T(8,128)S(1)} %pad_maximum_fusion), channel_id=1, source_target_pairs={{0,16},{16,32},{32,48},{48,64},{64,80},{80,96},{96,112},{112,128},... | collective-permute-start | bytes 737288 | tf_op jit(solution)/shard_map/ppermute | solution.py:11
  12.7 0.0 collective-permute-start.1
  12.7 3.1 %collective-permute-done = f32[15,16,256]{2,1,0:T(8,128)S(1)} collective-permute-done((f32[15,16,256]{2,1,0:T(8,128)S(1)}, f32[15,16,256]{2,1,0:T(8,128)S(1)}, u32[]{:S(2)}, u32[]{:S(2)}) %collective-permute-start) | collective-permute-done | bytes 245792 | tf_op jit(solution)/shard_map/ppermute | solution.py:11
  15.8 3.7 %collective-permute-done.1 = f32[15,16,256]{2,1,0:T(8,128)S(1)} collective-permute-done((f32[15,16,256]{2,1,0:T(8,128)S(1)}, f32[15,16,256]{2,1,0:T(8,128)S(1)}, u32[]{:S(2)}, u32[]{:S(2)}) %collective-permute-start.1) | collective-permute-done | bytes 245792 | tf_op jit(solution)/shard_map/ppermute | solution.py:11
  19.7 0.0 copy-done.2
  19.7 0.1 fusion.84
  19.8 0.0 copy-done.1
  19.8 0.1 bitcast_dynamic-update-slice_fusion
  20.0 66.8 %all-gather.3.cloned.1.call-done = f32[3,7,256,256]{3,2,1,0:T(8,128)} async-done(((f32[3,7,16,256]{3,2,1,0:T(8,128)}), f32[3,7,256,256]{3,2,1,0:T(8,128)}) %all-gather.3.cloned.1.call-update) | async-done | bytes 5505040 | tf_op jit(solution)/shard_map/all_gather | solution.py:74
  86.8 4.4 %fusion.16 = f32[3,7,16,256]{3,2,1,0:T(8,128)S(1)} fusion(f32[3,7,16,7,256]{4,2,3,1,0:T(8,128)S(1)} %fusion.68, f32[3,7,256,256]{3,2,1,0:T(8,128)} %all-gather.3.cloned.1.call-done, f32[3,7]{1,0:T(4,128)S(1)} %compare_convert_fusion), kind=kOutput, calls=%fused_computation.15 | convolution fusion | flops 926306304 | bytes 8257620 | tf_op jit(solution)/shard_map/ibcas,iasr->ibcr/dot_general | solution.py:65
  91.2 0.0 slice-start.1
  91.3 3.1 %collective-permute-start.2 = (f32[15,16,256]{2,1,0:T(8,128)S(1)}, f32[15,16,256]{2,1,0:T(8,128)S(1)}, u32[]{:S(2)}, u32[]{:S(2)}) collective-permute-start(f32[15,16,256]{2,1,0:T(8,128)S(1)} %pad_maximum_fusion.2), channel_id=1, source_target_pairs={{0,16},{16,32},{32,48},{48,64},{64,80},{80,96},{96,112},{112,128},... | collective-permute-start | bytes 737288 | tf_op jit(solution)/shard_map/ppermute | solution.py:11
  94.4 0.0 collective-permute-start.3
  94.4 3.1 %collective-permute-done.2 = f32[15,16,256]{2,1,0:T(8,128)S(1)} collective-permute-done((f32[15,16,256]{2,1,0:T(8,128)S(1)}, f32[15,16,256]{2,1,0:T(8,128)S(1)}, u32[]{:S(2)}, u32[]{:S(2)}) %collective-permute-start.2) | collective-permute-done | bytes 245792 | tf_op jit(solution)/shard_map/ppermute | solution.py:11
  97.7 3.5 %collective-permute-done.3 = f32[15,16,256]{2,1,0:T(8,128)S(1)} collective-permute-done((f32[15,16,256]{2,1,0:T(8,128)S(1)}, f32[15,16,256]{2,1,0:T(8,128)S(1)}, u32[]{:S(2)}, u32[]{:S(2)}) %collective-permute-start.3) | collective-permute-done | bytes 245792 | tf_op jit(solution)/shard_map/ppermute | solution.py:11
  101.3 0.1 fusion.83
  101.4 0.0 slice-done
  101.5 0.0 slice-done.1
  101.5 1.7 fusion.2
  103.2 0.8 fusion.80
  104.0 0.0 all-gather.5.cloned.1.call-update
  104.0 0.9 slice_bitcast_fusion.18
  105.0 1.0 slice_bitcast_fusion.10
  106.0 1.0 slice_bitcast_fusion.2
  106.9 0.2 collective-permute-start.4
  107.2 0.3 collective-permute-start.5
  107.5 2.8 %collective-permute-done.4 = f32[15,16,256]{2,1,0:T(8,128)S(1)} collective-permute-done((f32[15,16,256]{2,1,0:T(8,128)S(1)}, f32[15,16,256]{2,1,0:T(8,128)S(1)}, u32[]{:S(2)}, u32[]{:S(2)}) %collective-permute-start.4) | collective-permute-done | bytes 245792 | tf_op jit(solution)/shard_map/ppermute | solution.py:11
  110.3 3.7 %collective-permute-done.5 = f32[15,16,256]{2,1,0:T(8,128)S(1)} collective-permute-done((f32[15,16,256]{2,1,0:T(8,128)S(1)}, f32[15,16,256]{2,1,0:T(8,128)S(1)}, u32[]{:S(2)}, u32[]{:S(2)}) %collective-permute-start.5) | collective-permute-done | bytes 245792 | tf_op jit(solution)/shard_map/ppermute | solution.py:11
  114.2 0.0 copy-done
  114.2 0.1 fusion.82
  114.4 59.8 %all-gather.5.cloned.1.call-done = f32[3,7,256,256]{3,2,1,0:T(8,128)} async-done(((f32[3,7,16,256]{3,2,1,0:T(8,128)}), f32[3,7,256,256]{3,2,1,0:T(8,128)}) %all-gather.5.cloned.1.call-update) | async-done | bytes 5505040 | tf_op jit(solution)/shard_map/all_gather | solution.py:76
  174.2 4.4 %fusion.6 = f32[3,7,16,256,1]{3,2,0,1,4:T(8,128)S(1)} fusion(f32[3,7,16,7,256]{4,2,1,0,3:T(8,128)S(1)} %fusion.32, f32[3,7,256,256]{3,2,1,0:T(8,128)} %all-gather.5.cloned.1.call-done), kind=kOutput, calls=%fused_computation.6 | convolution fusion | flops 924844032 | bytes 8257536 | tf_op jit(solution)/shard_map/ibcas,iasr->ibcr/dot_general | solution.py:65
  178.7 0.1 bitcast_multiply_fusion.1
  178.8 0.0 slice-start.3
  178.9 3.1 %collective-permute-start.6 = (f32[15,16,256]{2,1,0:T(8,128)S(1)}, f32[15,16,256]{2,1,0:T(8,128)S(1)}, u32[]{:S(2)}, u32[]{:S(2)}) collective-permute-start(f32[15,16,256]{2,1,0:T(8,128)S(1)} %pad_maximum_fusion.6), channel_id=1, source_target_pairs={{0,16},{16,32},{32,48},{48,64},{64,80},{80,96},{96,112},{112,128},... | collective-permute-start | bytes 737288 | tf_op jit(solution)/shard_map/ppermute | solution.py:11
  181.9 0.0 collective-permute-start.7
  182.0 3.1 %collective-permute-done.6 = f32[15,16,256]{2,1,0:T(8,128)S(1)} collective-permute-done((f32[15,16,256]{2,1,0:T(8,128)S(1)}, f32[15,16,256]{2,1,0:T(8,128)S(1)}, u32[]{:S(2)}, u32[]{:S(2)}) %collective-permute-start.6) | collective-permute-done | bytes 245792 | tf_op jit(solution)/shard_map/ppermute | solution.py:11
  185.2 0.1 bitcast_dynamic-update-slice_fusion.1
  185.3 3.4 %collective-permute-done.7 = f32[15,16,256]{2,1,0:T(8,128)S(1)} collective-permute-done((f32[15,16,256]{2,1,0:T(8,128)S(1)}, f32[15,16,256]{2,1,0:T(8,128)S(1)}, u32[]{:S(2)}, u32[]{:S(2)}) %collective-permute-start.7) | collective-permute-done | bytes 245792 | tf_op jit(solution)/shard_map/ppermute | solution.py:11
  188.8 0.1 fusion.81
  189.0 1.8 fusion.4
  190.8 0.9 fusion.78
  (90 shorter events, 1.2 us)
Async XLA Ops:
  6.5 80.2 %all-gather.3.cloned.1.call-start = ((), (), s32[]{:S(2)}) async-start(), calls=%async_computation | async-start | bytes 5849088 | tf_op jit(solution)/shard_map/all_gather | solution.py:74
  7.3 167.0 %all-gather.5.cloned.1.call-start = ((), (), s32[]{:S(2)}) async-start(), calls=%async_computation.1 | async-start | bytes 5849088 | tf_op jit(solution)/shard_map/all_gather | solution.py:76
  9.2 10.5 %copy-start.2 = (pred[7]{0:T(512)(128)(4,1)S(1)}, pred[7]{0:T(512)(128)(4,1)}, u32[]{:S(2)}) copy-start(pred[7]{0:T(512)(128)(4,1)} %constant.7.clone.1) | copy-start | bytes 25
  9.2 6.6 %collective-permute-start = (f32[15,16,256]{2,1,0:T(8,128)S(1)}, f32[15,16,256]{2,1,0:T(8,128)S(1)}, u32[]{:S(2)}, u32[]{:S(2)}) collective-permute-start(f32[15,16,256]{2,1,0:T(8,128)S(1)} %pad_maximum_fusion), channel_id=1, source_target_pairs={{0,16},{16,32},{32,48},{48,64},{64,80},{80,96},{96,112},{112,128},... | collective-permute-start | bytes 737288 | tf_op jit(solution)/shard_map/ppermute | solution.py:11
  12.6 7.1 %copy-start.1 = (f32[3,7,16,256]{3,2,1,0:T(8,128)S(1)}, f32[3,7,16,256]{3,2,1,0:T(8,128)}, u32[]{:S(2)}) copy-start(f32[3,7,16,256]{3,2,1,0:T(8,128)} %param.2) | copy-start | bytes 1032196
  12.7 6.8 %collective-permute-start.1 = (f32[15,16,256]{2,1,0:T(8,128)S(1)}, f32[15,16,256]{2,1,0:T(8,128)S(1)}, u32[]{:S(2)}, u32[]{:S(2)}) collective-permute-start(f32[15,16,256]{2,1,0:T(8,128)S(1)} %pad_maximum_fusion.1), channel_id=1, source_target_pairs={{0,496},{16,0},{32,16},{48,32},{64,48},{80,64},{96,80},{112,96},{1... | collective-permute-start | bytes 737288 | tf_op jit(solution)/shard_map/ppermute | solution.py:11
  86.8 14.7 %slice-start = ((s8[5505024]{0:T(1024)(128)(4,1)}), s8[4194304]{0:T(1024)(128)(4,1)S(1)}, s32[]{:S(2)}) async-start(s8[5505024]{0:T(1024)(128)(4,1)} %bitcast.255), calls=%async_computation.2 | async-start | bytes 8388608
  91.2 10.2 %slice-start.1 = ((s8[5505024]{0:T(1024)(128)(4,1)}), s8[1310720]{0:T(1024)(128)(4,1)S(1)}, s32[]{:S(2)}) async-start(s8[5505024]{0:T(1024)(128)(4,1)} %bitcast.255), calls=%async_computation.3 | async-start | bytes 2621440
  91.3 6.2 %collective-permute-start.2 = (f32[15,16,256]{2,1,0:T(8,128)S(1)}, f32[15,16,256]{2,1,0:T(8,128)S(1)}, u32[]{:S(2)}, u32[]{:S(2)}) collective-permute-start(f32[15,16,256]{2,1,0:T(8,128)S(1)} %pad_maximum_fusion.2), channel_id=1, source_target_pairs={{0,16},{16,32},{32,48},{48,64},{64,80},{80,96},{96,112},{112,128},... | collective-permute-start | bytes 737288 | tf_op jit(solution)/shard_map/ppermute | solution.py:11
  94.4 6.8 %collective-permute-start.3 = (f32[15,16,256]{2,1,0:T(8,128)S(1)}, f32[15,16,256]{2,1,0:T(8,128)S(1)}, u32[]{:S(2)}, u32[]{:S(2)}) collective-permute-start(f32[15,16,256]{2,1,0:T(8,128)S(1)} %pad_maximum_fusion.3), channel_id=1, source_target_pairs={{0,496},{16,0},{32,16},{48,32},{64,48},{80,64},{96,80},{112,96},{1... | collective-permute-start | bytes 737288 | tf_op jit(solution)/shard_map/ppermute | solution.py:11
  104.0 10.1 %copy-start = (f32[3,7,16,256]{3,2,1,0:T(8,128)S(1)}, f32[3,7,16,256]{3,2,1,0:T(8,128)}, u32[]{:S(2)}) copy-start(f32[3,7,16,256]{3,2,1,0:T(8,128)} %fusion.80) | copy-start | bytes 1032196
  106.9 3.4 %collective-permute-start.4 = (f32[15,16,256]{2,1,0:T(8,128)S(1)}, f32[15,16,256]{2,1,0:T(8,128)S(1)}, u32[]{:S(2)}, u32[]{:S(2)}) collective-permute-start(f32[15,16,256]{2,1,0:T(8,128)S(1)} %pad_maximum_fusion.4), channel_id=1, source_target_pairs={{0,16},{16,32},{32,48},{48,64},{64,80},{80,96},{96,112},{112,128},... | collective-permute-start | bytes 737288 | tf_op jit(solution)/shard_map/ppermute | solution.py:11
  107.2 6.8 %collective-permute-start.5 = (f32[15,16,256]{2,1,0:T(8,128)S(1)}, f32[15,16,256]{2,1,0:T(8,128)S(1)}, u32[]{:S(2)}, u32[]{:S(2)}) collective-permute-start(f32[15,16,256]{2,1,0:T(8,128)S(1)} %pad_maximum_fusion.5), channel_id=1, source_target_pairs={{0,496},{16,0},{32,16},{48,32},{64,48},{80,64},{96,80},{112,96},{1... | collective-permute-start | bytes 737288 | tf_op jit(solution)/shard_map/ppermute | solution.py:11
  174.2 14.8 %slice-start.2 = ((s8[5505024]{0:T(1024)(128)(4,1)}), s8[4194304]{0:T(1024)(128)(4,1)S(1)}, s32[]{:S(2)}) async-start(s8[5505024]{0:T(1024)(128)(4,1)} %bitcast.257), calls=%async_computation.4 | async-start | bytes 8388608
  178.8 10.3 %slice-start.3 = ((s8[5505024]{0:T(1024)(128)(4,1)}), s8[1310720]{0:T(1024)(128)(4,1)S(1)}, s32[]{:S(2)}) async-start(s8[5505024]{0:T(1024)(128)(4,1)} %bitcast.257), calls=%async_computation.5 | async-start | bytes 2621440
  178.9 6.2 %collective-permute-start.6 = (f32[15,16,256]{2,1,0:T(8,128)S(1)}, f32[15,16,256]{2,1,0:T(8,128)S(1)}, u32[]{:S(2)}, u32[]{:S(2)}) collective-permute-start(f32[15,16,256]{2,1,0:T(8,128)S(1)} %pad_maximum_fusion.6), channel_id=1, source_target_pairs={{0,16},{16,32},{32,48},{48,64},{64,80},{80,96},{96,112},{112,128},... | collective-permute-start | bytes 737288 | tf_op jit(solution)/shard_map/ppermute | solution.py:11
  181.9 6.8 %collective-permute-start.7 = (f32[15,16,256]{2,1,0:T(8,128)S(1)}, f32[15,16,256]{2,1,0:T(8,128)S(1)}, u32[]{:S(2)}, u32[]{:S(2)}) collective-permute-start(f32[15,16,256]{2,1,0:T(8,128)S(1)} %pad_maximum_fusion.7), channel_id=1, source_target_pairs={{0,496},{16,0},{32,16},{48,32},{64,48},{80,64},{96,80},{112,96},{1... | collective-permute-start | bytes 737288 | tf_op jit(solution)/shard_map/ppermute | solution.py:11
Sparse Core Ops, SparseCore 0:
  10.4 76.3 all-gather.2
  104.2 70.0 all-gather.4
where the time goes:
time: 199 us; the launch traced here: 198 us
  waiting for transfers between devices  154 us (77%)
  between operations  14.1 us (7%)
  matrix products  12.3 us (6%)
  starting transfers between devices  10.2 us (5%)
  other arithmetic  4.81 us (2%)
  local copies, waits for them, and re-layouts  3.36 us (2%)
    all_gather x1, waiting for transfers between devices, on_device(): lax.all_gather(density, 'col', axis=2, tiled=True)  66.8 us
    all_gather x1, waiting for transfers between devices, on_device(): gathered, keep = (lax.all_gather(current, 'col', axis=2, tiled=True), None)  59.8 us
    ppermute x8, waiting for transfers between devices, send(): lax.ppermute(cells, 'blk', [(i, (i + shift) % count) for i in range(count)])  26.4 us
    dot_general x4, matrix products, contract(): jnp.einsum('ibcas,iasr->ibcr', stacked, shard_rows, precision=lax.Precisi...  12.3 us
    ppermute x8, starting transfers between devices, send(): lax.ppermute(cells, 'blk', [(i, (i + shift) % count) for i in range(count)])  10.1 us
  transfers between devices with their start and end apart: 10, of which 10 were waited for; matrix products, arithmetic and copies ran while one was open for 3% of the time, Pallas kernels for 0%

commit v1 on v0

--- a/solution.py
+++ b/solution.py
@@ -71,7 +71,18 @@
     current = density * pattern
     for purify_step in range(2):
         if purify_step == 0:
-            gathered, keep = (lax.all_gather(density, "col", axis=2, tiled=True), pattern)
+            gathered, keep = (
+                jnp.concatenate(
+                    jax.lax.all_to_all(
+                        jnp.stack([density for _ in range(jax.lax.psum(1, "col"))]),
+                        "col",
+                        split_axis=0,
+                        concat_axis=0,
+                    ),
+                    axis=2,
+                ),
+                pattern,
+            )
         else:
             gathered, keep = (lax.all_gather(current, "col", axis=2, tiled=True), None)
         square = contract(extend(current), gathered, keep) * pattern

time: 199 us -> 216 us (1.085)
  starting transfers between devices: 10.2 us -> 18.9 us
  local copies, waits for them, and re-layouts: 3.36 us -> 10.7 us
  waiting for transfers between devices: 154 us -> 158 us
    all_to_all x0 -> x1, waiting for transfers between devices: none -> 69.3 us  [on_device(): jax.lax.all_to_all(jnp.stack([density for _ in range(jax.lax.psum(1, 'col...]
    all_gather x1 -> x0, waiting for transfers between devices: 66.8 us -> none  [on_device(): lax.all_gather(density, 'col', axis=2, tiled=True)]
    all_to_all x0 -> x1, starting transfers between devices: none -> 6.93 us  [on_device(): jax.lax.all_to_all(jnp.stack([density for _ in range(jax.lax.psum(1, 'col...]
    another operation x0 -> x1, local copies, waits for them, and re-layouts: none -> 4.16 us  [on_device(): jnp.stack([density for _ in range(jax.lax.psum(1, 'col'))])]
    all_to_all x0 -> x1, local copies, waits for them, and re-layouts: none -> 3.18 us  [on_device(): jax.lax.all_to_all(jnp.stack([density for _ in range(jax.lax.psum(1, 'col...]
  transfers between devices with their start and end apart: 10 -> 10, of which waited for: 10 -> 10; matrix products, arithmetic and copies ran while one was open for 3% -> 2% of each run, Pallas kernels for 0% -> 0%
where the time goes in v1:
time: 216 us
  waiting for transfers between devices  158 us (73%)
  starting transfers between devices  18.9 us (9%)
  between operations  14.1 us (7%)
  local copies, waits for them, and re-layouts  10.7 us (5%)
  matrix products  10.3 us (5%)
  other arithmetic  4.15 us (2%)
    all_to_all x1, waiting for transfers between devices, on_device(): jax.lax.all_to_all(jnp.stack([density for _ in range(jax.lax.psum(1, 'col...  69.3 us
    all_gather x1, waiting for transfers between devices, on_device(): gathered, keep = (lax.all_gather(current, 'col', axis=2, tiled=True), None)  61.6 us
    ppermute x8, waiting for transfers between devices, send(): lax.ppermute(cells, 'blk', [(i, (i + shift) % count) for i in range(count)])  27 us
    ppermute x8, starting transfers between devices, send(): lax.ppermute(cells, 'blk', [(i, (i + shift) % count) for i in range(count)])  11.9 us
    dot_general x4, matrix products, contract(): jnp.einsum('ibcas,iasr->ibcr', stacked, shard_rows, precision=lax.Precisi...  10.3 us
    all_to_all x1, starting transfers between devices, on_device(): jax.lax.all_to_all(jnp.stack([density for _ in range(jax.lax.psum(1, 'col...  6.93 us
  transfers between devices with their start and end apart: 10, of which 10 were waited for; matrix products, arithmetic and copies ran while one was open for 2% of the time, Pallas kernels for 0%

profile of v1, /device:TPU:97, one launch (start us, length us, event | category | flops | bytes accessed | tf_op | source)
XLA Modules:
  0.0 216.1 jit_solution(17828560438047684979)
XLA Ops:
  6.5 4.2 %stack.227 = f32[16,3,7,16,256]{4,3,2,1,0:T(8,128)} broadcast(f32[3,7,16,256]{3,2,1,0:T(8,128)} %param.2), dimensions={1,2,3,4} | broadcast | bytes 5849088 | tf_op jit(solution)/shard_map/stack | solution.py:77
  10.7 6.9 %all-to-all-start = ((f32[16,3,7,16,256]{4,3,2,1,0:T(8,128)}), f32[16,3,7,16,256]{4,3,2,1,0:T(8,128)}, u32[]{:S(2)}, u32[]{:S(2)}) async-start(f32[16,3,7,16,256]{4,3,2,1,0:T(8,128)} %stack.227), calls=%async_computation | async-start | bytes 11010048 | tf_op jit(solution)/shard_map/all_to_all | solution.py:76
  17.6 0.0 all-gather.2.cloned.1.call-start
  17.7 0.0 copy-done.3
  17.7 0.1 compare_convert_fusion
  17.8 0.0 copy-done.1
  17.8 0.1 broadcast_multiply_fusion
  17.9 0.0 copy-start.2
  18.0 3.7 %collective-permute-start = (f32[15,16,256]{2,1,0:T(8,128)S(1)}, f32[15,16,256]{2,1,0:T(8,128)S(1)}, u32[]{:S(2)}, u32[]{:S(2)}) collective-permute-start(f32[15,16,256]{2,1,0:T(8,128)S(1)} %pad_maximum_fusion), channel_id=1, source_target_pairs={{0,16},{16,32},{32,48},{48,64},{64,80},{80,96},{96,112},{112,128},... | collective-permute-start | bytes 737288 | tf_op jit(solution)/shard_map/ppermute | solution.py:11
  21.7 0.0 collective-permute-start.1
  21.7 3.1 %collective-permute-done = f32[15,16,256]{2,1,0:T(8,128)S(1)} collective-permute-done((f32[15,16,256]{2,1,0:T(8,128)S(1)}, f32[15,16,256]{2,1,0:T(8,128)S(1)}, u32[]{:S(2)}, u32[]{:S(2)}) %collective-permute-start) | collective-permute-done | bytes 245792 | tf_op jit(solution)/shard_map/ppermute | solution.py:11
  24.9 4.1 %collective-permute-done.1 = f32[15,16,256]{2,1,0:T(8,128)S(1)} collective-permute-done((f32[15,16,256]{2,1,0:T(8,128)S(1)}, f32[15,16,256]{2,1,0:T(8,128)S(1)}, u32[]{:S(2)}, u32[]{:S(2)}) %collective-permute-start.1) | collective-permute-done | bytes 245792 | tf_op jit(solution)/shard_map/ppermute | solution.py:11
  29.1 0.0 copy-done.2
  29.1 0.1 fusion.97
  29.2 0.1 bitcast_dynamic-update-slice_fusion
  29.4 69.3 %all-to-all-done = f32[16,3,7,16,256]{4,3,2,1,0:T(8,128)} async-done(((f32[16,3,7,16,256]{4,3,2,1,0:T(8,128)}), f32[16,3,7,16,256]{4,3,2,1,0:T(8,128)}, u32[]{:S(2)}, u32[]{:S(2)}) %all-to-all-start) | async-done | bytes 5505056 | tf_op jit(solution)/shard_map/all_to_all | solution.py:76
  98.7 3.2 %copy.27 = f32[16,3,7,16,256]{4,3,0,2,1:T(8,128)S(1)} copy(f32[16,3,7,16,256]{4,3,2,1,0:T(8,128)} %all-to-all-done) | data formatting | bytes 11010048 | tf_op jit(solution)/shard_map/all_to_all | solution.py:76
  101.9 1.0 bitcast_multiply_fusion
  102.9 2.1 fusion.29
  105.1 4.6 %collective-permute-start.2 = (f32[15,16,256]{2,1,0:T(8,128)S(1)}, f32[15,16,256]{2,1,0:T(8,128)S(1)}, u32[]{:S(2)}, u32[]{:S(2)}) collective-permute-start(f32[15,16,256]{2,1,0:T(8,128)S(1)} %pad_maximum_fusion.2), channel_id=1, source_target_pairs={{0,16},{16,32},{32,48},{48,64},{64,80},{80,96},{96,112},{112,128},... | collective-permute-start | bytes 737288 | tf_op jit(solution)/shard_map/ppermute | solution.py:11
  109.7 0.0 collective-permute-start.3
  109.7 3.1 %collective-permute-done.2 = f32[15,16,256]{2,1,0:T(8,128)S(1)} collective-permute-done((f32[15,16,256]{2,1,0:T(8,128)S(1)}, f32[15,16,256]{2,1,0:T(8,128)S(1)}, u32[]{:S(2)}, u32[]{:S(2)}) %collective-permute-start.2) | collective-permute-done | bytes 245792 | tf_op jit(solution)/shard_map/ppermute | solution.py:11
  112.9 3.6 %collective-permute-done.3 = f32[15,16,256]{2,1,0:T(8,128)S(1)} collective-permute-done((f32[15,16,256]{2,1,0:T(8,128)S(1)}, f32[15,16,256]{2,1,0:T(8,128)S(1)}, u32[]{:S(2)}, u32[]{:S(2)}) %collective-permute-start.3) | collective-permute-done | bytes 245792 | tf_op jit(solution)/shard_map/ppermute | solution.py:11
  116.7 0.1 fusion.96
  116.9 2.1 fusion.21
  118.9 0.8 fusion.93
  119.8 0.0 all-gather.2.cloned.1.call-update
  119.8 0.9 slice_bitcast_fusion.18
  120.7 1.0 slice_bitcast_fusion.10
  121.7 1.0 slice_bitcast_fusion.2
  122.7 0.1 collective-permute-start.4
  122.8 0.4 collective-permute-start.5
  123.3 2.7 %collective-permute-done.4 = f32[15,16,256]{2,1,0:T(8,128)S(1)} collective-permute-done((f32[15,16,256]{2,1,0:T(8,128)S(1)}, f32[15,16,256]{2,1,0:T(8,128)S(1)}, u32[]{:S(2)}, u32[]{:S(2)}) %collective-permute-start.4) | collective-permute-done | bytes 245792 | tf_op jit(solution)/shard_map/ppermute | solution.py:11
  126.0 3.7 %collective-permute-done.5 = f32[15,16,256]{2,1,0:T(8,128)S(1)} collective-permute-done((f32[15,16,256]{2,1,0:T(8,128)S(1)}, f32[15,16,256]{2,1,0:T(8,128)S(1)}, u32[]{:S(2)}, u32[]{:S(2)}) %collective-permute-start.5) | collective-permute-done | bytes 245792 | tf_op jit(solution)/shard_map/ppermute | solution.py:11
  129.8 0.0 copy-done
  129.9 0.1 fusion.95
  130.1 61.6 %all-gather.2.cloned.1.call-done = f32[3,7,256,256]{3,2,1,0:T(8,128)} async-done(((f32[3,7,16,256]{3,2,1,0:T(8,128)}), f32[3,7,256,256]{3,2,1,0:T(8,128)}) %all-gather.2.cloned.1.call-update) | async-done | bytes 5505040 | tf_op jit(solution)/shard_map/all_gather | solution.py:87
  191.6 4.4 %fusion.11 = f32[3,7,16,256]{3,2,0,1:T(8,128)S(1)} fusion(f32[3,7,16,7,256]{4,2,1,0,3:T(8,128)S(1)} %fusion.45, f32[3,7,256,256]{3,2,1,0:T(8,128)} %all-gather.2.cloned.1.call-done), kind=kOutput, calls=%fused_computation.12 | convolution fusion | flops 924844032 | bytes 8257536 | tf_op jit(solution)/shard_map/ibcas,iasr->ibcr/dot_general | solution.py:65
  196.1 0.1 copy_multiply_fusion.1
  196.2 0.0 slice-start.1
  196.3 3.1 %collective-permute-start.6 = (f32[15,16,256]{2,1,0:T(8,128)S(1)}, f32[15,16,256]{2,1,0:T(8,128)S(1)}, u32[]{:S(2)}, u32[]{:S(2)}) collective-permute-start(f32[15,16,256]{2,1,0:T(8,128)S(1)} %pad_maximum_fusion.6), channel_id=1, source_target_pairs={{0,16},{16,32},{32,48},{48,64},{64,80},{80,96},{96,112},{112,128},... | collective-permute-start | bytes 737288 | tf_op jit(solution)/shard_map/ppermute | solution.py:11
  199.3 0.0 collective-permute-start.7
  199.4 3.1 %collective-permute-done.6 = f32[15,16,256]{2,1,0:T(8,128)S(1)} collective-permute-done((f32[15,16,256]{2,1,0:T(8,128)S(1)}, f32[15,16,256]{2,1,0:T(8,128)S(1)}, u32[]{:S(2)}, u32[]{:S(2)}) %collective-permute-start.6) | collective-permute-done | bytes 245792 | tf_op jit(solution)/shard_map/ppermute | solution.py:11
  202.5 3.6 %collective-permute-done.7 = f32[15,16,256]{2,1,0:T(8,128)S(1)} collective-permute-done((f32[15,16,256]{2,1,0:T(8,128)S(1)}, f32[15,16,256]{2,1,0:T(8,128)S(1)}, u32[]{:S(2)}, u32[]{:S(2)}) %collective-permute-start.7) | collective-permute-done | bytes 245792 | tf_op jit(solution)/shard_map/ppermute | solution.py:11
  206.3 0.1 bitcast_dynamic-update-slice_fusion.1
  206.4 0.1 fusion.94
  206.6 1.8 fusion.16
  208.4 0.9 fusion.91
  (89 shorter events, 1.2 us)
Async XLA Ops:
  10.7 7.0 %copy-start.3 = (s32[3]{0:T(128)S(1)}, s32[3]{0:T(128)}, u32[]{:S(2)}) copy-start(s32[3]{0:T(128)} %param.3) | copy-start | bytes 40
  10.7 7.1 %copy-start.1 = (f32[3,7,16,256]{3,2,1,0:T(8,128)S(1)}, f32[3,7,16,256]{3,2,1,0:T(8,128)}, u32[]{:S(2)}) copy-start(f32[3,7,16,256]{3,2,1,0:T(8,128)} %param.2) | copy-start | bytes 1032196
  10.7 88.0 %all-to-all-start = ((f32[16,3,7,16,256]{4,3,2,1,0:T(8,128)}), f32[16,3,7,16,256]{4,3,2,1,0:T(8,128)}, u32[]{:S(2)}, u32[]{:S(2)}) async-start(f32[16,3,7,16,256]{4,3,2,1,0:T(8,128)} %stack.227), calls=%async_computation | async-start | bytes 11010048 | tf_op jit(solution)/shard_map/all_to_all | solution.py:76
  17.6 174.0 %all-gather.2.cloned.1.call-start = ((), (), s32[]{:S(2)}) async-start(), calls=%async_computation.1 | async-start | bytes 5849088 | tf_op jit(solution)/shard_map/all_gather | solution.py:87
  17.9 11.2 %copy-start.2 = (pred[7]{0:T(512)(128)(4,1)S(1)}, pred[7]{0:T(512)(128)(4,1)}, u32[]{:S(2)}) copy-start(pred[7]{0:T(512)(128)(4,1)} %constant.7.clone.1) | copy-start | bytes 25
  18.0 6.8 %collective-permute-start = (f32[15,16,256]{2,1,0:T(8,128)S(1)}, f32[15,16,256]{2,1,0:T(8,128)S(1)}, u32[]{:S(2)}, u32[]{:S(2)}) collective-permute-start(f32[15,16,256]{2,1,0:T(8,128)S(1)} %pad_maximum_fusion), channel_id=1, source_target_pairs={{0,16},{16,32},{32,48},{48,64},{64,80},{80,96},{96,112},{112,128},... | collective-permute-start | bytes 737288 | tf_op jit(solution)/shard_map/ppermute | solution.py:11
  21.7 7.2 %collective-permute-start.1 = (f32[15,16,256]{2,1,0:T(8,128)S(1)}, f32[15,16,256]{2,1,0:T(8,128)S(1)}, u32[]{:S(2)}, u32[]{:S(2)}) collective-permute-start(f32[15,16,256]{2,1,0:T(8,128)S(1)} %pad_maximum_fusion.1), channel_id=1, source_target_pairs={{0,496},{16,0},{32,16},{48,32},{64,48},{80,64},{96,80},{112,96},{1... | collective-permute-start | bytes 737288 | tf_op jit(solution)/shard_map/ppermute | solution.py:11
  105.1 7.7 %collective-permute-start.2 = (f32[15,16,256]{2,1,0:T(8,128)S(1)}, f32[15,16,256]{2,1,0:T(8,128)S(1)}, u32[]{:S(2)}, u32[]{:S(2)}) collective-permute-start(f32[15,16,256]{2,1,0:T(8,128)S(1)} %pad_maximum_fusion.2), channel_id=1, source_target_pairs={{0,16},{16,32},{32,48},{48,64},{64,80},{80,96},{96,112},{112,128},... | collective-permute-start | bytes 737288 | tf_op jit(solution)/shard_map/ppermute | solution.py:11
  109.7 6.8 %collective-permute-start.3 = (f32[15,16,256]{2,1,0:T(8,128)S(1)}, f32[15,16,256]{2,1,0:T(8,128)S(1)}, u32[]{:S(2)}, u32[]{:S(2)}) collective-permute-start(f32[15,16,256]{2,1,0:T(8,128)S(1)} %pad_maximum_fusion.3), channel_id=1, source_target_pairs={{0,496},{16,0},{32,16},{48,32},{64,48},{80,64},{96,80},{112,96},{1... | collective-permute-start | bytes 737288 | tf_op jit(solution)/shard_map/ppermute | solution.py:11
  119.8 10.0 %copy-start = (f32[3,7,16,256]{3,2,1,0:T(8,128)S(1)}, f32[3,7,16,256]{3,2,1,0:T(8,128)}, u32[]{:S(2)}) copy-start(f32[3,7,16,256]{3,2,1,0:T(8,128)} %fusion.93) | copy-start | bytes 1032196
  122.7 3.2 %collective-permute-start.4 = (f32[15,16,256]{2,1,0:T(8,128)S(1)}, f32[15,16,256]{2,1,0:T(8,128)S(1)}, u32[]{:S(2)}, u32[]{:S(2)}) collective-permute-start(f32[15,16,256]{2,1,0:T(8,128)S(1)} %pad_maximum_fusion.4), channel_id=1, source_target_pairs={{0,16},{16,32},{32,48},{48,64},{64,80},{80,96},{96,112},{112,128},... | collective-permute-start | bytes 737288 | tf_op jit(solution)/shard_map/ppermute | solution.py:11
  122.8 6.8 %collective-permute-start.5 = (f32[15,16,256]{2,1,0:T(8,128)S(1)}, f32[15,16,256]{2,1,0:T(8,128)S(1)}, u32[]{:S(2)}, u32[]{:S(2)}) collective-permute-start(f32[15,16,256]{2,1,0:T(8,128)S(1)} %pad_maximum_fusion.5), channel_id=1, source_target_pairs={{0,496},{16,0},{32,16},{48,32},{64,48},{80,64},{96,80},{112,96},{1... | collective-permute-start | bytes 737288 | tf_op jit(solution)/shard_map/ppermute | solution.py:11
  191.6 15.0 %slice-start = ((s8[5505024]{0:T(1024)(128)(4,1)}), s8[4194304]{0:T(1024)(128)(4,1)S(1)}, s32[]{:S(2)}) async-start(s8[5505024]{0:T(1024)(128)(4,1)} %bitcast.249), calls=%async_computation.2 | async-start | bytes 8388608
  196.2 10.5 %slice-start.1 = ((s8[5505024]{0:T(1024)(128)(4,1)}), s8[1310720]{0:T(1024)(128)(4,1)S(1)}, s32[]{:S(2)}) async-start(s8[5505024]{0:T(1024)(128)(4,1)} %bitcast.249), calls=%async_computation.3 | async-start | bytes 2621440
  196.3 6.2 %collective-permute-start.6 = (f32[15,16,256]{2,1,0:T(8,128)S(1)}, f32[15,16,256]{2,1,0:T(8,128)S(1)}, u32[]{:S(2)}, u32[]{:S(2)}) collective-permute-start(f32[15,16,256]{2,1,0:T(8,128)S(1)} %pad_maximum_fusion.6), channel_id=1, source_target_pairs={{0,16},{16,32},{32,48},{48,64},{64,80},{80,96},{96,112},{112,128},... | collective-permute-start | bytes 737288 | tf_op jit(solution)/shard_map/ppermute | solution.py:11
  199.3 6.8 %collective-permute-start.7 = (f32[15,16,256]{2,1,0:T(8,128)S(1)}, f32[15,16,256]{2,1,0:T(8,128)S(1)}, u32[]{:S(2)}, u32[]{:S(2)}) collective-permute-start(f32[15,16,256]{2,1,0:T(8,128)S(1)} %pad_maximum_fusion.7), channel_id=1, source_target_pairs={{0,496},{16,0},{32,16},{48,32},{64,48},{80,64},{96,80},{112,96},{1... | collective-permute-start | bytes 737288 | tf_op jit(solution)/shard_map/ppermute | solution.py:11
Sparse Core Ops, SparseCore 0:
  119.9 71.6 all-gather.1
